TPU v7x, 512 devices: a whole 4x8x8 slice. The times are simulated.
512 devices in a mesh: expert: 64 (over x, z, core), group: 8 (over y).
Axes of the slice: x: 4, y: 8, z: 8, core: 2. Of those that a mesh axis runs over, the one named last changes fastest.
Arguments:
- tokens: bfloat16 [4096, 4096], P('expert', 'group'), may hold values from -6 to 6
- gate_weight: bfloat16 [64, 1536, 4096], P('expert', 'group'), may hold values from -0.09375 to 0.09375
- up_weight: bfloat16 [64, 1536, 4096], P('expert', 'group'), may hold values from -0.09375 to 0.09375
- down_weight: bfloat16 [64, 1536, 4096], P('expert', 'group'), may hold values from -0.15625 to 0.15625
- expert_ids: int32 [4096, 8], P('expert'), may hold values from 0 to 63, all different within a row; in each aligned block of 64 rows (0 to 63, 64 to 127, ...) at most 12 rows name the same one
- gate_scores: bfloat16 [4096, 8], P('expert'), may hold values from 0.19921875 to 1
Outputs:
- mixed: bfloat16 [4096, 4096], P('expert', 'group')
Inputs may be any that keep to these rules, and one draw needn't show every extreme that they name: `expert_ids`: the 8 experts of a token are distinct; within the 64 rows of one device no expert is named by more than 12 rows, a bound that some block reaches.
All inputs are finite; a program needn't handle non-finite values.
Results may differ from a plain program's by a relative error of at most 0.019.
Values may be sent and summed in bfloat16 or wider, within the bound.
No kernel may reach another device: no remote copies, remote signals or barrier semaphores. Data moves between devices by JAX's collectives and lax.ppermute only.
A program may use at most 128 MiB of HBM per device.

v0:
```python
import jax
import jax.numpy as jnp
from jax import lax
from jax.sharding import PartitionSpec as P


def route_tables(expert_ids, gate_scores, experts):
    tok_rows, top_count = expert_ids.shape
    capacity = tok_rows * top_count * 3 // (2 * experts)
    flat_ids = expert_ids.reshape(-1)
    onehot = (flat_ids[:, None] == jnp.arange(experts, dtype=jnp.int32)[None, :]).astype(jnp.int32)
    before = jnp.cumsum(onehot, axis=0) - onehot
    slot_index = jnp.sum(before * onehot, axis=1).reshape(tok_rows, top_count)
    slot_keys = expert_ids * capacity + slot_index
    columns = jnp.arange(experts * capacity, dtype=jnp.int32)
    matches = slot_keys[:, :, None] == columns[None, None, :]
    selector = jnp.any(matches, axis=1).astype(jnp.bfloat16)
    weights = jnp.sum(
        jnp.where(matches, gate_scores[:, :, None].astype(jnp.float32), 0.0), axis=1
    ).astype(jnp.bfloat16)
    return (capacity, selector, weights)


def per_device(tokens, gate_weight, up_weight, down_weight, expert_ids, gate_scores):
    experts = lax.axis_size("expert")
    capacity, selector, weights = route_tables(expert_ids, gate_scores, experts)
    placed = lax.dot_general(
        selector, tokens, (((0,), (0,)), ((), ())), preferred_element_type=jnp.float32
    ).astype(jnp.bfloat16)
    arrived = lax.all_to_all(
        placed.reshape(experts, capacity, tokens.shape[1]), "expert", 0, 0, tiled=True
    ).reshape(experts * capacity, tokens.shape[1])
    row_block = lax.all_gather(arrived, "group", axis=1, tiled=True)
    gate_value = lax.dot_general(
        row_block, gate_weight[0], (((1,), (1,)), ((), ())), preferred_element_type=jnp.float32
    )
    up_value = lax.dot_general(
        row_block, up_weight[0], (((1,), (1,)), ((), ())), preferred_element_type=jnp.float32
    )
    hidden = (jax.nn.silu(gate_value) * up_value).astype(jnp.bfloat16)
    hidden_all = lax.all_gather(hidden, "group", axis=1, tiled=True)
    down_cols = lax.all_to_all(down_weight[0], "group", 1, 0, tiled=True)
    partial_value = jnp.dot(hidden_all, down_cols, preferred_element_type=jnp.float32)
    returned = lax.all_to_all(
        partial_value.astype(jnp.bfloat16).reshape(experts, capacity, -1),
        "expert",
        0,
        0,
        tiled=True,
    ).reshape(experts * capacity, -1)
    combined = jnp.dot(weights, returned, preferred_element_type=jnp.float32)
    return combined.astype(jnp.bfloat16)


def solution(mesh):
    placed = (
        P("expert", "group"),
        P("expert", "group", None),
        P("expert", "group", None),
        P("expert", "group", None),
        P("expert", None),
        P("expert", None),
    )
    return jax.shard_map(
        per_device, mesh=mesh, in_specs=placed, out_specs=P("expert", "group"), check_vma=False
    )
```

profile of v0, /device:TPU:1, one launch (start us, length us, event | category | flops | bytes accessed | tf_op | source)
XLA Modules:
  0.0 261.2 jit_solution(7376772480139769284)
XLA Ops:
  6.5 0.9 copy.36
  7.6 1.2 reduce-window.6
  8.8 0.2 slice_reduce_fusion
  9.1 0.1 fusion.13
  9.4 0.7 multiply_add_fusion
  10.2 0.5 fusion.4
  10.7 1.3 convolution_convert_fusion
  12.0 0.2 reshape.41
  12.2 43.3 %all_to_all.29 = bf16[64,12,512]{2,1,0:T(8,128)(2,1)} all-to-all(bf16[64,12,512]{2,1,0:T(8,128)(2,1)S(1)} %reshape.41), channel_id=1, replica_groups=mesh['expert'=64,'group'=8] {'expert'}, dimensions={0} | all-to-all | bytes 1572864 | tf_op jit(solution)/shard_map/all_to_all | solution.py:30
  55.4 2.1 reshape.42
  57.6 73.5 %all-gather.3.cloned.1.call-done = bf16[768,4096]{1,0:T(8,128)(2,1)} async-done(((bf16[768,512]{1,0:T(8,128)(2,1)}), bf16[768,4096]{1,0:T(8,128)(2,1)}) %all-gather.3.cloned.1.call-update) | async-done | bytes 6291472 | tf_op jit(solution)/shard_map/all_gather | solution.py:33
  131.1 5.2 %fusion.2 = f32[768,192]{0,1:T(8,128)S(1)} fusion(bf16[768,4096]{1,0:T(8,128)(2,1)} %all-gather.3.cloned.1.call-done, bf16[1,192,4096]{2,1,0:T(8,128)(2,1)S(1)} %copy-done), kind=kOutput, calls=%fused_computation.2 | convolution fusion | flops 1207959552 | bytes 8454144 | tf_op jit(solution)/shard_map/dot_general | solution.py:34
  136.3 4.5 %fusion.8 = bf16[768,192]{0,1:T(8,128)(2,1)} fusion(bf16[768,4096]{1,0:T(8,128)(2,1)S(1)} %copy-done.3, bf16[1,192,4096]{2,1,0:T(8,128)(2,1)} %param.8, f32[768,192]{0,1:T(8,128)S(1)} %fusion.2), kind=kOutput, calls=%fused_computation.10 | convolution fusion | flops 1208844288 | bytes 8749056 | tf_op jit(solution)/shard_map/dot_general | solution.py:37
  140.8 0.6 copy.44
  141.5 0.5 copy.42
  142.0 55.0 %all_to_all.30 = bf16[192,8,512]{2,0,1:T(8,128)(2,1)S(1)} all-to-all(bf16[192,8,512]{2,0,1:T(8,128)(2,1)S(1)} %copy.42), channel_id=1, replica_groups=mesh['expert'=64,'group'=8] {'group'}, dimensions={1} | all-to-all | bytes 3145728 | tf_op jit(solution)/shard_map/all_to_all | solution.py:42
  197.0 9.2 %all-gather.5.cloned.1.call-done = bf16[768,1536]{0,1:T(8,128)(2,1)} async-done(((bf16[768,192]{0,1:T(8,128)(2,1)}), bf16[768,1536]{0,1:T(8,128)(2,1)}) %all-gather.5.cloned.1.call-update) | async-done | bytes 2359312 | tf_op jit(solution)/shard_map/all_gather | solution.py:41
  206.2 4.0 %convolution_convert_fusion.1 = bf16[768,512]{1,0:T(8,128)(2,1)} fusion(bf16[768,1536]{0,1:T(8,128)(2,1)} %all-gather.5.cloned.1.call-done, bf16[1536,512]{1,0:T(8,128)(2,1)S(1)} %bitcast.45), kind=kOutput, calls=%fused_computation.8 | convolution fusion | flops 1208352768 | bytes 4718592 | tf_op jit(solution)/shard_map/dot_general | solution.py:43
  210.2 2.1 reshape.43
  212.3 12.4 %all-to-all-start.2 = ((bf16[64,12,512]{2,1,0:T(8,128)(2,1)}), bf16[64,12,512]{2,1,0:T(8,128)(2,1)S(1)}, u32[]{:S(2)}, u32[]{:S(2)}) async-start(bf16[64,12,512]{2,1,0:T(8,128)(2,1)} %reshape.43), calls=%async_computation.2 | async-start | bytes 2097152 | tf_op jit(solution)/shard_map/all_to_all | solution.py:44
  224.8 0.6 select_reduce_fusion
  225.4 27.9 %all-to-all-done.2 = bf16[64,12,512]{2,1,0:T(8,128)(2,1)S(1)} async-done(((bf16[64,12,512]{2,1,0:T(8,128)(2,1)}), bf16[64,12,512]{2,1,0:T(8,128)(2,1)S(1)}, u32[]{:S(2)}, u32[]{:S(2)}) %all-to-all-start.2) | async-done | bytes 786464 | tf_op jit(solution)/shard_map/all_to_all | solution.py:44
  253.3 0.2 reshape.44
  253.4 0.9 convolution_convert_fusion.2
  (21 shorter events, 0.7 us)
Async XLA Ops:
  6.5 124.6 %copy-start = (bf16[1,192,4096]{2,1,0:T(8,128)(2,1)S(1)}, bf16[1,192,4096]{2,1,0:T(8,128)(2,1)}, u32[]{:S(2)}) copy-start(bf16[1,192,4096]{2,1,0:T(8,128)(2,1)} %param.7) | copy-start | bytes 4718596
  6.5 124.6 %all-gather.3.cloned.1.call-start = ((), (), s32[]{:S(2)}) async-start(), calls=%async_computation.3 | async-start | bytes 7077888 | tf_op jit(solution)/shard_map/all_gather | solution.py:33
  57.5 148.7 %all-gather.5.cloned.1.call-start = ((), (), s32[]{:S(2)}) async-start(), calls=%async_computation.4 | async-start | bytes 2654208 | tf_op jit(solution)/shard_map/all_gather | solution.py:41
  131.1 5.2 %copy-start.3 = (bf16[768,4096]{1,0:T(8,128)(2,1)S(1)}, bf16[768,4096]{1,0:T(8,128)(2,1)}, u32[]{:S(2)}) copy-start(bf16[768,4096]{1,0:T(8,128)(2,1)} %all-gather.3.cloned.1.call-done) | copy-start | bytes 18874372
  136.3 4.5 %copy-start.1 = (bf16[1,192,4096]{2,1,0:T(8,128)(2,1)S(1)}, bf16[1,192,4096]{2,1,0:T(8,128)(2,1)}, u32[]{:S(2)}) copy-start(bf16[1,192,4096]{2,1,0:T(8,128)(2,1)} %param.9) | copy-start | bytes 4718596
  210.2 14.6 %copy-start.2 = (bf16[64,8]{0,1:T(8,128)(2,1)S(1)}, bf16[64,8]{0,1:T(8,128)(2,1)}, u32[]{:S(2)}) copy-start(bf16[64,8]{0,1:T(8,128)(2,1)} %param.11) | copy-start | bytes 3076
  212.3 41.0 %all-to-all-start.2 = ((bf16[64,12,512]{2,1,0:T(8,128)(2,1)}), bf16[64,12,512]{2,1,0:T(8,128)(2,1)S(1)}, u32[]{:S(2)}, u32[]{:S(2)}) async-start(bf16[64,12,512]{2,1,0:T(8,128)(2,1)} %reshape.43), calls=%async_computation.2 | async-start | bytes 2097152 | tf_op jit(solution)/shard_map/all_to_all | solution.py:44
Sparse Core Ops, SparseCore 0:
  57.7 73.4 all-gather.2
  140.9 65.2 all-gather.4
where the time goes:
time: 262 us; the launch traced here: 261 us
  waiting for transfers between devices  111 us (42%)
  blocking collectives  98.3 us (38%)
  matrix products  15.8 us (6%)
  between operations  13.5 us (5%)
  starting transfers between devices  12.5 us (5%)
  local copies, waits for them, and re-layouts  7.35 us (3%)
  other arithmetic  3.17 us (1%)
    all_gather x1, waiting for transfers between devices, per_device(): row_block = lax.all_gather(arrived, 'group', axis=1, tiled=True)  73.5 us
    all_to_all x1, blocking collectives, per_device(): down_cols = lax.all_to_all(down_weight[0], 'group', 1, 0, tiled=True)  55 us
    all_to_all x1, blocking collectives, per_device(): lax.all_to_all(placed.reshape(experts, capacity, tokens.shape[1]), 'exper...  43.3 us
    all_to_all x1, waiting for transfers between devices, per_device(): lax.all_to_all(partial_value.astype(jnp.bfloat16).reshape(experts, capaci...  27.9 us
    all_to_all x1, starting transfers between devices, per_device(): lax.all_to_all(partial_value.astype(jnp.bfloat16).reshape(experts, capaci...  12.4 us
    all_gather x1, waiting for transfers between devices, per_device(): hidden_all = lax.all_gather(hidden, 'group', axis=1, tiled=True)  9.22 us
  transfers between devices with their start and end apart: 3, of which 3 were waited for; matrix products, arithmetic and copies ran while one was open for 1% of the time, Pallas kernels for 0%

commit v1 on v0

--- a/solution.py
+++ b/solution.py
@@ -38,7 +38,9 @@
         row_block, up_weight[0], (((1,), (1,)), ((), ())), preferred_element_type=jnp.float32
     )
     hidden = (jax.nn.silu(gate_value) * up_value).astype(jnp.bfloat16)
-    hidden_all = lax.all_gather(hidden, "group", axis=1, tiled=True)
+    hidden_all = jnp.concatenate(
+        lax.all_to_all(jnp.stack([hidden] * lax.axis_size("group")), "group", 0, 0), axis=1
+    )
     down_cols = lax.all_to_all(down_weight[0], "group", 1, 0, tiled=True)
     partial_value = jnp.dot(hidden_all, down_cols, preferred_element_type=jnp.float32)
     returned = lax.all_to_all(

time: 262 us -> 281 us (1.073)
  waiting for transfers between devices: 111 us -> 125 us
  blocking collectives: 98.3 us -> 103 us
  matrix products: 15.8 us -> 11.9 us
    all_gather x1, waiting for transfers between devices: 73.5 us -> 97.3 us  [per_device(): row_block = lax.all_gather(arrived, 'group', axis=1, tiled=True)]
    all_gather x1 -> x0, waiting for transfers between devices: 9.22 us -> none  [per_device(): hidden_all = lax.all_gather(hidden, 'group', axis=1, tiled=True)]
    all_to_all x0 -> x1, starting transfers between devices: none -> 6.82 us  [per_device(): down_cols = lax.all_to_all(down_weight[0], 'group', 1, 0, tiled=True)]
    all_to_all x1, blocking collectives: 55 us -> 59.7 us  [per_device(): lax.all_to_all(jnp.stack([hidden] * lax.axis_size('group')), 'group', 0, 0)]
    all_to_all x1, starting transfers between devices: 12.4 us -> 7.72 us  [per_device(): lax.all_to_all(partial_value.astype(jnp.bfloat16).reshape(experts, capaci...]
  transfers between devices with their start and end apart: 3 -> 3, of which waited for: 3 -> 2; matrix products, arithmetic and copies ran while one was open for 1% -> 4% of each run, Pallas kernels for 0% -> 0%
where the time goes in v1:
time: 281 us; the launch traced here: 280 us
  waiting for transfers between devices  125 us (44%)
  blocking collectives  103 us (37%)
  starting transfers between devices  14.5 us (5%)
  between operations  13.5 us (5%)
  matrix products  11.9 us (4%)
  local copies, waits for them, and re-layouts  8.82 us (3%)
  other arithmetic  3.17 us (1%)
    all_gather x1, waiting for transfers between devices, per_device(): row_block = lax.all_gather(arrived, 'group', axis=1, tiled=True)  97.3 us
    all_to_all x1, blocking collectives, per_device(): lax.all_to_all(jnp.stack([hidden] * lax.axis_size('group')), 'group', 0, 0)  59.7 us
    all_to_all x1, blocking collectives, per_device(): lax.all_to_all(placed.reshape(experts, capacity, tokens.shape[1]), 'exper...  43.3 us
    all_to_all x1, waiting for transfers between devices, per_device(): lax.all_to_all(partial_value.astype(jnp.bfloat16).reshape(experts, capaci...  27.9 us
    all_to_all x1, starting transfers between devices, per_device(): lax.all_to_all(partial_value.astype(jnp.bfloat16).reshape(experts, capaci...  7.72 us
    all_to_all x1, starting transfers between devices, per_device(): down_cols = lax.all_to_all(down_weight[0], 'group', 1, 0, tiled=True)  6.82 us
  transfers between devices with their start and end apart: 3, of which 2 were waited for; matrix products, arithmetic and copies ran while one was open for 4% of the time, Pallas kernels for 0%

profile of v1, /device:TPU:1, one launch (start us, length us, event | category | flops | bytes accessed | tf_op | source)
XLA Modules:
  0.0 280.1 jit_solution(8050337429065673999)
XLA Ops:
  6.5 0.9 copy.23
  7.6 1.2 reduce-window.6
  8.8 0.2 slice_reduce_fusion
  9.4 0.7 multiply_add_fusion
  10.2 0.5 fusion.7
  10.7 1.3 convolution_convert_fusion
  12.0 0.2 reshape.47
  12.2 43.3 %all_to_all.31 = bf16[64,12,512]{2,1,0:T(8,128)(2,1)} all-to-all(bf16[64,12,512]{2,1,0:T(8,128)(2,1)S(1)} %reshape.47), channel_id=1, replica_groups=mesh['expert'=64,'group'=8] {'expert'}, dimensions={0} | all-to-all | bytes 1572864 | tf_op jit(solution)/shard_map/all_to_all | solution.py:30
  55.4 2.2 reshape.48
  57.7 0.6 copy.31
  58.4 1.6 copy.29
  60.0 6.8 %all-to-all-start.2 = ((bf16[192,8,512]{2,0,1:T(8,128)(2,1)}), bf16[192,8,512]{2,0,1:T(8,128)(2,1)S(1)}, u32[]{:S(2)}, u32[]{:S(2)}) async-start(bf16[192,8,512]{2,0,1:T(8,128)(2,1)} %copy.29), calls=%async_computation.2 | async-start | bytes 3145728 | tf_op jit(solution)/shard_map/all_to_all | solution.py:44
  66.8 97.3 %all-gather.2.cloned.1.call-done = bf16[768,4096]{1,0:T(8,128)(2,1)} async-done(((bf16[768,512]{1,0:T(8,128)(2,1)}), bf16[768,4096]{1,0:T(8,128)(2,1)}) %all-gather.2.cloned.1.call-update) | async-done | bytes 6291472 | tf_op jit(solution)/shard_map/all_gather | solution.py:33
  164.1 5.1 %fusion.5 = f32[768,192]{0,1:T(8,128)S(1)} fusion(bf16[768,4096]{1,0:T(8,128)(2,1)} %all-gather.2.cloned.1.call-done, bf16[1,192,4096]{2,1,0:T(8,128)(2,1)S(1)} %copy-done), kind=kOutput, calls=%fused_computation.6 | convolution fusion | flops 1207959552 | bytes 8454144 | tf_op jit(solution)/shard_map/dot_general | solution.py:34
  169.3 2.2 fusion.15
  171.6 0.2 stack.2
  171.7 59.7 %all_to_all.32 = bf16[8,768,192]{1,2,0:T(8,128)(2,1)S(1)} all-to-all(bf16[8,768,192]{1,2,0:T(8,128)(2,1)S(1)} %stack.2), channel_id=1, replica_groups=mesh['expert'=64,'group'=8] {'group'}, dimensions={0} | all-to-all | bytes 4718592 | tf_op jit(solution)/shard_map/all_to_all | solution.py:42
  231.5 2.3 bitcast_convert_fusion
  233.8 2.1 reshape.50
  235.9 7.7 %all-to-all-start.3 = ((bf16[64,12,512]{2,1,0:T(8,128)(2,1)}), bf16[64,12,512]{2,1,0:T(8,128)(2,1)S(1)}, u32[]{:S(2)}, u32[]{:S(2)}) async-start(bf16[64,12,512]{2,1,0:T(8,128)(2,1)} %reshape.50), calls=%async_computation.3 | async-start | bytes 2097152 | tf_op jit(solution)/shard_map/all_to_all | solution.py:46
  243.8 0.6 select_reduce_fusion
  244.3 27.9 %all-to-all-done.3 = bf16[64,12,512]{2,1,0:T(8,128)(2,1)S(1)} async-done(((bf16[64,12,512]{2,1,0:T(8,128)(2,1)}), bf16[64,12,512]{2,1,0:T(8,128)(2,1)S(1)}, u32[]{:S(2)}, u32[]{:S(2)}) %all-to-all-start.3) | async-done | bytes 786464 | tf_op jit(solution)/shard_map/all_to_all | solution.py:46
  272.2 0.2 reshape.51
  272.4 0.9 convolution_convert_fusion.1
  (23 shorter events, 0.7 us)
Async XLA Ops:
  6.5 157.6 %copy-start = (bf16[1,192,4096]{2,1,0:T(8,128)(2,1)S(1)}, bf16[1,192,4096]{2,1,0:T(8,128)(2,1)}, u32[]{:S(2)}) copy-start(bf16[1,192,4096]{2,1,0:T(8,128)(2,1)} %param.7) | copy-start | bytes 4718596
  6.5 157.6 %all-gather.2.cloned.1.call-start = ((), (), s32[]{:S(2)}) async-start(), calls=%async_computation.4 | async-start | bytes 7077888 | tf_op jit(solution)/shard_map/all_gather | solution.py:33
  55.4 2.3 copy-start.1
  60.0 111.6 %all-to-all-start.2 = ((bf16[192,8,512]{2,0,1:T(8,128)(2,1)}), bf16[192,8,512]{2,0,1:T(8,128)(2,1)S(1)}, u32[]{:S(2)}, u32[]{:S(2)}) async-start(bf16[192,8,512]{2,0,1:T(8,128)(2,1)} %copy.29), calls=%async_computation.2 | async-start | bytes 3145728 | tf_op jit(solution)/shard_map/all_to_all | solution.py:44
  164.1 5.2 %copy-start.3 = (bf16[768,4096]{1,0:T(8,128)(2,1)S(1)}, bf16[768,4096]{1,0:T(8,128)(2,1)}, u32[]{:S(2)}) copy-start(bf16[768,4096]{1,0:T(8,128)(2,1)} %all-gather.2.cloned.1.call-done) | copy-start | bytes 18874372
  164.1 5.2 %copy-start.4 = (bf16[1,192,4096]{2,1,0:T(8,128)(2,1)S(1)}, bf16[1,192,4096]{2,1,0:T(8,128)(2,1)}, u32[]{:S(2)}) copy-start(bf16[1,192,4096]{2,1,0:T(8,128)(2,1)} %param.8) | copy-start | bytes 4718596
  233.8 9.9 %copy-start.2 = (bf16[64,8]{0,1:T(8,128)(2,1)S(1)}, bf16[64,8]{0,1:T(8,128)(2,1)}, u32[]{:S(2)}) copy-start(bf16[64,8]{0,1:T(8,128)(2,1)} %param.11) | copy-start | bytes 3076
  235.9 36.3 %all-to-all-start.3 = ((bf16[64,12,512]{2,1,0:T(8,128)(2,1)}), bf16[64,12,512]{2,1,0:T(8,128)(2,1)S(1)}, u32[]{:S(2)}, u32[]{:S(2)}) async-start(bf16[64,12,512]{2,1,0:T(8,128)(2,1)} %reshape.50), calls=%async_computation.3 | async-start | bytes 2097152 | tf_op jit(solution)/shard_map/all_to_all | solution.py:46
Sparse Core Ops, SparseCore 0:
  57.8 106.2 all-gather.1
